TPU v7x, 256 devices: a whole 4x4x8 slice. The times are simulated.
256 devices in a mesh: ctx: 8 (over z), head: 16 (over y, x), req: 2 (over core).
Axes of the slice: x: 4, y: 4, z: 8, core: 2. Of those that a mesh axis runs over, the one named last changes fastest.
Arguments:
- x_in: bfloat16 [2, 8192, 16384], P('req', 'ctx', 'head'), may hold values from -6 to 6
- bc_in: bfloat16 [2, 8192, 4096], P('req', 'ctx'), may hold values from -0.625 to 0.625
- z_in: bfloat16 [2, 8192, 16384], P('req', 'ctx', 'head'), may hold values from -6 to 6
- dt_raw: float32 [2, 256, 8192], P('req', 'head', 'ctx'), may hold values from -6 to 6
- dt_bias: float32 [256], P('head'), may hold values from -3 to 1
- decay_rate: float32 [256], P('head'), may hold values from 1e-06 to 0.05
- skip_gain: float32 [256], P('head'), may hold values from 0.5 to 1.5
- conv_x: float32 [4, 16384], P(None, 'head'), may hold values from -3 to 3
- conv_bc: float32 [4, 4096], replicated, may hold values from -3 to 3
- ssm_pool: float32 [16, 256, 64, 256], P(('ctx', 'req'), 'head'), may hold values from -6 to 6
- conv_pool: float32 [16, 3, 16384], P(('ctx', 'req'), None, 'head'), may hold values from -6 to 6
- bc_cache: float32 [2, 3, 4096], P('req'), may hold values from -0.625 to 0.625
- owner: int32 [2, 16], P(None, 'head'), may hold values from 0 to 15, as said below
- lengths: int32 [2], replicated, may hold values from 2048 to 8192, as said below
Outputs:
- y_out: bfloat16 [2, 8192, 16384], P('req', 'ctx', 'head')
- block_states: float32 [2, 8, 256, 64, 256], P('req', 'ctx', 'head')
Inputs may be any that keep to these rules, and one draw needn't show every extreme that they name: `owner`: for every head block the requests' cached states lie in different slots. `lengths`: one request has all 8192 new tokens.
All inputs are finite; a program needn't handle non-finite values.
Results may differ from a plain program's by a relative error of at most 0.0053.
Values may be sent and summed in bfloat16 or wider, within the bound.
No kernel may reach another device: no remote copies, remote signals or barrier semaphores. Data moves between devices by JAX's collectives and lax.ppermute only.
A program may use at most 128 MiB of HBM per device.

v0:
```python
from functools import partial
import jax
import jax.numpy as jnp
from jax import lax
from jax.sharding import PartitionSpec as P

H = 256
P_SIZE = 64
N = 256
G = 8
K = 4
STRETCH = 256
CHUNKS = 4
HIGHEST = lax.Precision.HIGHEST


def passed_along(value, axis, steps):
    count = lax.axis_size(axis)
    initial, last = (max(0, -steps), min(count, count - steps))
    return lax.ppermute(value, axis, [(source, source + steps) for source in range(initial, last)])


def causal_conv(prev_rows, rows, taps):
    padded = jnp.concatenate([prev_rows, rows.astype(jnp.float32)], axis=0)
    count = rows.shape[0]
    total = taps[0] * padded[0:count]
    for offset in range(1, taps.shape[0]):
        total = total + taps[offset] * padded[offset : offset + count]
    return jax.nn.silu(total).astype(jnp.bfloat16)


def block_state(running, x_blk, b_blk, step_blk, cum):
    block_len, head_count = (x_blk.shape[0], x_blk.shape[1])
    group_count = b_blk.shape[1]
    per_group = head_count // group_count
    block_end = cum[:, -1:]
    factor = step_blk * jnp.exp(-(block_end - cum))
    weighted = (x_blk.astype(jnp.float32) * factor.T[:, :, None]).astype(jnp.bfloat16)
    weighted_view = weighted.reshape(block_len, group_count, per_group, running.shape[1])
    contrib = jnp.einsum(
        "qgjp,qgn->gjpn", weighted_view, b_blk, preferred_element_type=jnp.float32
    ).reshape(running.shape)
    return jnp.exp(-cum[:, -1])[:, None, None] * running + contrib


def block_output(running, x_blk, b_blk, c_blk, step_blk, cum, skip_gain):
    block_len = x_blk.shape[0]
    head_count = x_blk.shape[1]
    scores = jnp.einsum("qgn,sgn->gqs", c_blk, b_blk, preferred_element_type=jnp.float32)
    group_count = scores.shape[0]
    per_group = head_count // group_count
    scores_h = jnp.broadcast_to(
        scores[:, None], (group_count, per_group, block_len, block_len)
    ).reshape(head_count, block_len, block_len)
    row_ids = lax.broadcasted_iota(jnp.int32, (block_len, block_len), 0)
    col_ids = lax.broadcasted_iota(jnp.int32, (block_len, block_len), 1)
    causal = (row_ids >= col_ids)[None]
    decay_gap = jnp.where(causal, cum[:, :, None] - cum[:, None, :], 0.0)
    decay_mask = jnp.where(causal, jnp.exp(-decay_gap), 0.0)
    weights = (scores_h * decay_mask * step_blk[:, None, :]).astype(jnp.bfloat16)
    y_intra = jnp.einsum("hqs,shp->qhp", weights, x_blk, preferred_element_type=jnp.float32)
    state_view = running.reshape(group_count, per_group, running.shape[1], running.shape[2])
    y_state = jnp.einsum("qgn,gjpn->qgjp", c_blk.astype(jnp.float32), state_view, precision=HIGHEST)
    y_state = y_state.reshape(block_len, head_count, running.shape[1]) * jnp.exp(-cum).T[:, :, None]
    return y_intra + y_state + skip_gain[None, :, None] * x_blk.astype(jnp.float32)


def on_device(
    x_in,
    bc_in,
    z_in,
    dt_raw,
    dt_bias,
    decay_rate,
    skip_gain,
    conv_x,
    conv_bc,
    ssm_pool,
    conv_pool,
    bc_cache,
    owner,
    lengths,
):
    n_ctx = lax.axis_size("ctx")
    n_req = lax.axis_size("req")
    ctx_pos = lax.axis_index("ctx")
    head_pos = lax.axis_index("head")
    req_pos = lax.axis_index("req")
    local_heads = dt_raw.shape[1]
    tokens = x_in.shape[1]
    at_start = ctx_pos == 0
    want = owner[req_pos, 0]
    on_chip = want // n_req == ctx_pos
    mine = want % n_req == req_pos
    swap = [(src, n_req - 1 - src) for src in range(n_req)]
    other_pool, other_conv = lax.ppermute((ssm_pool[0], conv_pool[0]), "req", swap)
    state_pick = jnp.where(on_chip, jnp.where(mine, ssm_pool[0], other_pool), 0.0)
    conv_pick = jnp.where(on_chip, jnp.where(mine, conv_pool[0], other_conv), 0.0)
    picked = jnp.concatenate([state_pick.reshape(-1), conv_pick.reshape(-1)])
    picked, x_in, bc_in, dt_raw = lax.optimization_barrier((picked, x_in, bc_in, dt_raw))
    picked = lax.psum(picked, "ctx")
    first_state = picked[: state_pick.size].reshape(state_pick.shape)
    first_conv = picked[state_pick.size :].reshape(conv_pick.shape)
    tail_x = x_in[0, tokens - (K - 1) :, :]
    tail_bc = bc_in[0, tokens - (K - 1) :, :]
    prev_x, prev_bc = passed_along((tail_x, tail_bc), "ctx", 1)
    prev_x = jnp.where(at_start, first_conv, prev_x.astype(jnp.float32))
    prev_bc = jnp.where(at_start, bc_cache[0], prev_bc.astype(jnp.float32))
    per_group = H // G
    local_groups = max(1, local_heads // per_group)
    group_start = head_pos * local_heads // per_group
    span = local_groups * N

    def pick_groups(values):
        input_cols = lax.dynamic_slice_in_dim(values, group_start * N, span, 1)
        output_cols = lax.dynamic_slice_in_dim(values, G * N + group_start * N, span, 1)
        return jnp.concatenate([input_cols, output_cols], axis=1)

    x_head = causal_conv(prev_x, x_in[0, : K - 1], conv_x)
    x_rest = causal_conv(x_in[0, : K - 1].astype(jnp.float32), x_in[0, K - 1 :], conv_x)
    x_conv = jnp.concatenate([x_head, x_rest], axis=0)
    bc_conv = causal_conv(pick_groups(prev_bc), pick_groups(bc_in[0]), pick_groups(conv_bc))
    positions = ctx_pos * tokens + lax.iota(jnp.int32, tokens)
    live_mask = (positions < lengths[req_pos]).astype(jnp.float32)
    step_size = jax.nn.softplus(dt_raw[0] + dt_bias[:, None]) * live_mask[None, :]
    log_decay = step_size * decay_rate[:, None]
    blocks = tokens // STRETCH
    x_view = x_conv.reshape(blocks, STRETCH, local_heads, P_SIZE)
    b_view = bc_conv[:, :span].reshape(blocks, STRETCH, local_groups, N)
    c_view = bc_conv[:, span:].reshape(blocks, STRETCH, local_groups, N)
    step_view = step_size.reshape(local_heads, blocks, STRETCH).transpose(1, 0, 2)
    log_view = log_decay.reshape(local_heads, blocks, STRETCH).transpose(1, 0, 2)
    cum_view = jnp.cumsum(log_view, axis=2)
    running = jnp.zeros((local_heads, P_SIZE, N), jnp.float32)
    starts = []
    for blk in range(blocks):
        starts.append(running)
        running = block_state(running, x_view[blk], b_view[blk], step_view[blk], cum_view[blk])
    local_end = running
    own_decay = jnp.exp(-jnp.sum(log_decay, axis=1))
    chunk = local_heads // CHUNKS
    end_chunks = local_end.reshape(CHUNKS, chunk, P_SIZE, N)
    init_chunks = first_state.reshape(CHUNKS, chunk, P_SIZE, N)
    decay_chunks = own_decay.reshape(CHUNKS, chunk)
    got = jnp.zeros((chunk, P_SIZE, N), jnp.float32)
    received = []
    for step in range(n_ctx + CHUNKS - 2):
        index = jnp.clip(step - ctx_pos, 0, CHUNKS - 1)
        prior = jnp.where(
            at_start, lax.dynamic_index_in_dim(init_chunks, index, keepdims=False), got
        )
        sent = lax.dynamic_index_in_dim(decay_chunks, index, keepdims=False)[
            :, None, None
        ] * prior + lax.dynamic_index_in_dim(end_chunks, index, keepdims=False)
        pairs = [
            (src, src + 1) for src in range(max(0, step - CHUNKS + 1), min(step, n_ctx - 2) + 1)
        ]
        got = lax.ppermute(sent, "ctx", pairs)
        received.append(got)
    received = jnp.stack(received)
    prefix = lax.dynamic_slice_in_dim(received, jnp.maximum(ctx_pos - 1, 0), CHUNKS, 0)
    start_state = jnp.where(at_start, first_state, prefix.reshape(local_heads, P_SIZE, N))
    end_state = own_decay[:, None, None] * start_state + local_end
    outs = []
    for blk in range(blocks):
        outs.append(
            block_output(
                starts[blk],
                x_view[blk],
                b_view[blk],
                c_view[blk],
                step_view[blk],
                cum_view[blk],
                skip_gain,
            )
        )
    local_out = jnp.concatenate(outs, axis=0)
    cum_dev = jnp.cumsum(log_decay, axis=1)
    readout = bc_conv[:, span:].reshape(tokens, local_groups, N)
    start_view = start_state.reshape(local_groups, local_heads // local_groups, P_SIZE, N)
    carried = jnp.einsum(
        "tgn,gjpn->tgjp", readout.astype(jnp.float32), start_view, precision=HIGHEST
    )
    carried = carried.reshape(tokens, local_heads, P_SIZE) * jnp.exp(-cum_dev).T[:, :, None]
    mixed = local_out + carried
    gate_act = jax.nn.silu(z_in[0].astype(jnp.float32)).reshape(tokens, local_heads, P_SIZE)
    gated = (
        (mixed * gate_act * live_mask[:, None, None])
        .reshape(1, tokens, local_heads * P_SIZE)
        .astype(jnp.bfloat16)
    )
    return (gated, end_state[None, None])


def solution(mesh):
    return jax.shard_map(
        on_device,
        mesh=mesh,
        in_specs=(
            P("req", "ctx", "head"),
            P("req", "ctx", None),
            P("req", "ctx", "head"),
            P("req", "head", "ctx"),
            P("head"),
            P("head"),
            P("head"),
            P(None, "head"),
            P(),
            P(("ctx", "req"), "head", None, None),
            P(("ctx", "req"), None, "head"),
            P("req", None, None),
            P(None, "head"),
            P(),
        ),
        out_specs=(P("req", "ctx", "head"), P("req", "ctx", "head", None, None)),
        check_vma=False,
    )
```

profile of v0, /device:TPU:232, one launch (start us, length us, event | category | flops | bytes accessed | tf_op | source)
XLA Modules:
  0.0 251.9 jit_solution(4440000627590166594)
XLA Ops:
  19.1 3.9 %copy.78 = bf16[1,1024,1024]{1,2,0:T(8,128)(2,1)} copy(bf16[1,1024,1024]{2,1,0:T(8,128)(2,1)} %param.16) | data formatting | bytes 4194304 | tf_op args[2]
  27.7 2.9 %copy.66 = bf16[1,1024,1024]{1,2,0:T(8,128)(2,1)S(1)} copy(bf16[1,1024,1024]{2,1,0:T(8,128)(2,1)} %param.14) | data formatting | bytes 4194304 | tf_op jit(solution)/shard_map/optimization_barrier | solution.py:100
  32.2 2.3 reduce-window.14
  42.7 3.0 %fusion.21 = f32[1021,1024]{0,1:T(8,128)} fusion(bf16[1,1024,1024]{1,2,0:T(8,128)(2,1)S(1)} %copy.66), kind=kLoop, calls=%fused_computation.38 | loop fusion | flops 1045504 | bytes 6273024 | tf_op jit(solution)/shard_map/convert_element_type | solution.py:24
  48.2 11.3 %multiply_convert_fusion.4 = bf16[1021,1024]{0,1:T(8,128)(2,1)S(1)} fusion(f32[1021,1024]{0,1:T(8,128)} %fusion.21, f32[3,1024]{0,1:T(8,128)} %copy.67, f32[1024]{0:T(1024)S(1)} %bitcast.440, f32[1024]{0:T(1024)S(1)} %bitcast.442, f32[1024]{0:T(1024)S(1)} %bitcast.438, f32[1024]{0:T(1024)S(1)} %bitcast.436), kind=kLoop, calls=%fused_computation.24 | loop fusion | flops 15682560 | bytes 6301696 | tf_op jit(solution)/shard_map/convert_element_type | solution.py:29
  59.5 1.9 fusion.148
  62.4 4.5 %reduce-window.16 = f32[16,8,128]{2,1,0:T(8,128)S(1)} reduce-window(f32[16,8,128]{2,1,0:T(8,128)S(1)} %fusion.116, f32[]{:T(128)} %constant.162.clone.1), window={size=1x1x128 pad=0_0x0_0x127_0}, to_apply=%region_4.5 | reduce-window | flops 2080768 | bytes 131076 | tf_op jit(solution)/shard_map/reduce-window.2
  72.3 1.9 pad_maximum_fusion.1
  76.5 50.6 %all-reduce.2.cloned.1.call-done = f32[265216]{0:T(1024)} async-done(((f32[265216]{0:T(1024)}), f32[265216]{0:T(1024)}) %all-reduce.2.cloned.1.call-update) | async-done | bytes 1060880 | tf_op jit(solution)/shard_map/psum | solution.py:101
  129.4 2.9 %fusion.65 = (bf16[256,1024]{0,1:T(8,128)(2,1)S(1)}, bf16[256,1024]{0,1:T(8,128)(2,1)}, bf16[256,1024]{0,1:T(8,128)(2,1)S(1)}, bf16[256,1024]{0,1:T(8,128)(2,1)S(1)}, bf16[256,1024]{0,1:T(8,128)(2,1)S(1)}) fusion(f32[256,16]{0,1:T(8,128)S(1)} %get-tuple-element.52, bf16[1021,1024]{0,1:T(8,128)(2,1)S(1)} %multiply_convert_fusion.4, ...), kind=kLoop, calls=%fused_computation.94 | loop fusion | flops 4194304 | bytes 6619136 | tf_op jit(solution)/shard_map/convert_element_type | solution.py:38
  137.0 2.1 multiply_add_fusion
  142.5 2.6 %fusion.47 = f32[256,16,64]{0,2,1:T(8,128)} fusion(bf16[256,16,64]{0,2,1:T(8,128)(2,1)S(1)} %bitcast.410, f32[16,256]{1,0:T(8,128)S(1)} %copy-done.54, f32[16,256]{1,0:T(8,128)S(1)} %bitcast.433, f32[256,256]{1,0:T(8,128)S(1)} %fusion.97, pred[256,256]{1,0:T(8,128)(4,1)S(1)} %copy-done.37), kind=kOutput, calls=%fused_computation.65 | convolution fusion | flops 141557760 | bytes 1933312 | tf_op jit(solution)/shard_map/hqs,shp->qhp/dot_general | solution.py:61
  146.4 2.6 %fusion.46 = f32[256,16,64]{0,2,1:T(8,128)} fusion(bf16[256,16,64]{0,2,1:T(8,128)(2,1)S(1)} %bitcast.414, f32[16,256]{1,0:T(8,128)S(1)} %copy-done.52, f32[16,256]{1,0:T(8,128)S(1)} %bitcast.429, f32[256,256]{1,0:T(8,128)S(1)} %fusion.92, pred[256,256]{1,0:T(8,128)(4,1)S(1)} %copy-done.37), kind=kOutput, calls=%fused_computation.64 | convolution fusion | flops 141557760 | bytes 1933312 | tf_op jit(solution)/shard_map/hqs,shp->qhp/dot_general | solution.py:61
  152.3 1.8 fusion.59
  156.4 1.7 fusion.58
  158.0 2.5 slice.267
  165.1 42.8 %collective-permute-done.10 = f32[4,64,256]{2,1,0:T(8,128)S(1)} collective-permute-done((f32[4,64,256]{2,1,0:T(8,128)S(1)}, f32[4,64,256]{2,1,0:T(8,128)S(1)}, u32[]{:S(2)}, u32[]{:S(2)}) %collective-permute-start.10) | collective-permute-done | bytes 262176 | tf_op jit(solution)/shard_map/ppermute | solution.py:158
  211.6 6.3 %collective-permute-done.11 = f32[4,64,256]{2,1,0:T(8,128)S(1)} collective-permute-done((f32[4,64,256]{2,1,0:T(8,128)S(1)}, f32[4,64,256]{2,1,0:T(8,128)S(1)}, u32[]{:S(2)}, u32[]{:S(2)}) %collective-permute-start.11) | collective-permute-done | bytes 262176 | tf_op jit(solution)/shard_map/ppermute | solution.py:158
  220.3 6.0 %collective-permute-done.12 = f32[4,64,256]{2,1,0:T(8,128)S(1)} collective-permute-done((f32[4,64,256]{2,1,0:T(8,128)S(1)}, f32[4,64,256]{2,1,0:T(8,128)S(1)}, u32[]{:S(2)}, u32[]{:S(2)}) %collective-permute-start.12) | collective-permute-done | bytes 262176 | tf_op jit(solution)/shard_map/ppermute | solution.py:158
  227.8 6.9 %collective-permute-done.13 = f32[4,64,256]{2,1,0:T(8,128)S(1)} collective-permute-done((f32[4,64,256]{2,1,0:T(8,128)S(1)}, f32[4,64,256]{2,1,0:T(8,128)S(1)}, u32[]{:S(2)}, u32[]{:S(2)}) %collective-permute-start.13) | collective-permute-done | bytes 262176 | tf_op jit(solution)/shard_map/ppermute | solution.py:158
  234.9 1.6 add_bitcast_fusion
  236.5 1.8 fusion.67
  240.6 1.9 fusion.13
  242.5 2.6 %copy.79 = bf16[1,1024,1024]{2,1,0:T(8,128)(2,1)} copy(bf16[1,1024,1024]{1,2,0:T(8,128)(2,1)S(1)} %fusion.13) | data formatting | bytes 4194304
  (306 shorter events, 65.2 us)
Async XLA Ops:
  7.2 119.9 %all-reduce.2.cloned.1.call-start = ((), (), s32[]{:S(2)}) async-start(), calls=%async_computation | async-start | bytes 2121728 | tf_op jit(solution)/shard_map/psum | solution.py:101
  7.2 15.8 %collective-permute-start = (f32[16,64,256]{2,1,0:T(8,128)}, f32[16,64,256]{2,1,0:T(8,128)S(1)}, u32[]{:S(2)}, u32[]{:S(2)}) collective-permute-start(f32[16,64,256]{2,1,0:T(8,128)} %bitcast.416), channel_id=1, source_target_pairs={{0,1},{1,0},{2,3},{3,2},{4,5},{5,4},{6,7},{7,6},{8,9},{9,8},{10,11... | collective-permute-start | bytes 3145736 | tf_op jit(solution)/shard_map/ppermute | solution.py:96
  8.1 14.9 %collective-permute-start.1 = (f32[3,1024]{1,0:T(4,128)S(1)}, f32[3,1024]{1,0:T(4,128)S(1)}, u32[]{:S(2)}, u32[]{:S(2)}) collective-permute-start(f32[3,1024]{1,0:T(4,128)S(1)} %bitcast.445), channel_id=1, source_target_pairs={{0,1},{1,0},{2,3},{3,2},{4,5},{5,4},{6,7},{7,6},{8,9},{9,8},{10,11... | collective-permute-start | bytes 36872 | tf_op jit(solution)/shard_map/ppermute | solution.py:96
  26.1 41.2 %copy-start.11 = (bf16[1024,256]{1,0:T(8,128)(2,1)}, bf16[1024,256]{1,0:T(8,128)(2,1)S(1)}, u32[]{:S(2)}) copy-start(bf16[1024,256]{1,0:T(8,128)(2,1)S(1)} %get-tuple-element.27) | copy-start | bytes 1572868
  26.2 41.2 %copy-start.13 = (bf16[1024,256]{1,0:T(8,128)(2,1)}, bf16[1024,256]{1,0:T(8,128)(2,1)S(1)}, u32[]{:S(2)}) copy-start(bf16[1024,256]{1,0:T(8,128)(2,1)S(1)} %get-tuple-element.28) | copy-start | bytes 1572868
  41.4 30.8 %collective-permute-start.3 = (bf16[3,4096]{1,0:T(4,128)(2,1)}, bf16[3,4096]{1,0:T(4,128)(2,1)S(1)}, u32[]{:S(2)}, u32[]{:S(2)}) collective-permute-start(bf16[3,4096]{1,0:T(4,128)(2,1)} %slice_bitcast_fusion.3), channel_id=1, source_target_pairs={{0,32},{32,64},{64,96},{96,128},{128,160},{160,192},{192,224},{1,3... | collective-permute-start | bytes 73736 | tf_op jit(solution)/shard_map/ppermute | solution.py:20
  46.7 81.2 %collective-permute-start.2 = (bf16[3,1024]{1,0:T(4,128)(2,1)}, bf16[3,1024]{1,0:T(4,128)(2,1)S(1)}, u32[]{:S(2)}, u32[]{:S(2)}) collective-permute-start(bf16[3,1024]{1,0:T(4,128)(2,1)} %get-tuple-element.35), channel_id=1, source_target_pairs={{0,32},{32,64},{64,96},{96,128},{128,160},{160,192},{192,224},{1,3... | collective-permute-start | bytes 18440 | tf_op jit(solution)/shard_map/ppermute | solution.py:20
  75.4 58.8 %copy-start.4 = (bf16[1024,512]{1,0:T(8,128)(2,1)}, bf16[1024,512]{1,0:T(8,128)(2,1)S(1)}, u32[]{:S(2)}) copy-start(bf16[1024,512]{1,0:T(8,128)(2,1)S(1)} %multiply_convert_fusion.9) | copy-start | bytes 3145732
  139.2 2.4 collective-permute-start.4
  141.7 3.5 %collective-permute-start.5 = (f32[4,64,256]{2,1,0:T(8,128)S(1)}, f32[4,64,256]{2,1,0:T(8,128)S(1)}, u32[]{:S(2)}, u32[]{:S(2)}) collective-permute-start(f32[4,64,256]{2,1,0:T(8,128)S(1)} %bitcast_add_fusion.8), channel_id=1, source_target_pairs={{0,32},{32,64},{1,33},{33,65},{2,34},{34,66},{3,35},{35,67},{4,36}... | collective-permute-start | bytes 786440 | tf_op jit(solution)/shard_map/ppermute | solution.py:158
  145.4 3.8 %collective-permute-start.6 = (f32[4,64,256]{2,1,0:T(8,128)S(1)}, f32[4,64,256]{2,1,0:T(8,128)S(1)}, u32[]{:S(2)}, u32[]{:S(2)}) collective-permute-start(f32[4,64,256]{2,1,0:T(8,128)S(1)} %bitcast_add_fusion.7), channel_id=1, source_target_pairs={{0,32},{32,64},{64,96},{1,33},{33,65},{65,97},{2,34},{34,66},{66,9... | collective-permute-start | bytes 786440 | tf_op jit(solution)/shard_map/ppermute | solution.py:158
  149.3 2.2 collective-permute-start.7
  151.6 2.5 %collective-permute-start.8 = (f32[4,64,256]{2,1,0:T(8,128)S(1)}, f32[4,64,256]{2,1,0:T(8,128)S(1)}, u32[]{:S(2)}, u32[]{:S(2)}) collective-permute-start(f32[4,64,256]{2,1,0:T(8,128)S(1)} %bitcast_add_fusion.5), channel_id=1, source_target_pairs={{32,64},{64,96},{96,128},{128,160},{33,65},{65,97},{97,129},{129,1... | collective-permute-start | bytes 786440 | tf_op jit(solution)/shard_map/ppermute | solution.py:158
  154.2 53.8 %copy-start.73 = (f32[4]{0:T(128)S(1)}, f32[4]{0:T(128)}, u32[]{:S(2)}) copy-start(f32[4]{0:T(128)} %get-tuple-element.69) | copy-start | bytes 52
  155.0 5.6 %collective-permute-start.9 = (f32[4,64,256]{2,1,0:T(8,128)}, f32[4,64,256]{2,1,0:T(8,128)}, u32[]{:S(2)}, u32[]{:S(2)}) collective-permute-start(f32[4,64,256]{2,1,0:T(8,128)} %bitcast_add_fusion.4), channel_id=1, source_target_pairs={{64,96},{96,128},{128,160},{160,192},{65,97},{97,129},{129,161},{1... | collective-permute-start | bytes 786440 | tf_op jit(solution)/shard_map/ppermute | solution.py:158
  156.3 61.6 %copy-start.72 = (f32[4]{0:T(128)S(1)}, f32[4]{0:T(128)}, u32[]{:S(2)}) copy-start(f32[4]{0:T(128)} %get-tuple-element.68) | copy-start | bytes 52
  158.0 68.3 %copy-start.71 = (f32[4]{0:T(128)S(1)}, f32[4]{0:T(128)}, u32[]{:S(2)}) copy-start(f32[4]{0:T(128)} %get-tuple-element.67) | copy-start | bytes 52
  160.5 51.0 %copy-start.29 = (f32[4,64,256]{2,1,0:T(8,128)S(1)}, f32[4,64,256]{2,1,0:T(8,128)}, u32[]{:S(2)}) copy-start(f32[4,64,256]{2,1,0:T(8,128)} %copy-done.28) | copy-start | bytes 786436
  160.6 57.4 %copy-start.3 = (f32[4,4,64,256]{3,2,1,0:T(8,128)S(1)}, f32[4,4,64,256]{3,2,1,0:T(8,128)}, u32[]{:S(2)}) copy-start(f32[4,4,64,256]{3,2,1,0:T(8,128)} %reshape_reshape.3) | copy-start | bytes 3145732
  161.8 46.1 %collective-permute-start.10 = (f32[4,64,256]{2,1,0:T(8,128)S(1)}, f32[4,64,256]{2,1,0:T(8,128)S(1)}, u32[]{:S(2)}, u32[]{:S(2)}) collective-permute-start(f32[4,64,256]{2,1,0:T(8,128)S(1)} %bitcast_add_fusion.3), channel_id=1, source_target_pairs={{96,128},{128,160},{160,192},{192,224},{97,129},{129,161},{161,193... | collective-permute-start | bytes 786440 | tf_op jit(solution)/shard_map/ppermute | solution.py:158
  208.9 25.8 %copy-start.8 = (f32[16,64,256]{2,1,0:T(8,128)S(1)}, f32[16,64,256]{2,1,0:T(8,128)}, u32[]{:S(2)}) copy-start(f32[16,64,256]{2,1,0:T(8,128)} %fusion.85) | copy-start | bytes 3145732
  209.0 8.9 %collective-permute-start.11 = (f32[4,64,256]{2,1,0:T(8,128)S(1)}, f32[4,64,256]{2,1,0:T(8,128)S(1)}, u32[]{:S(2)}, u32[]{:S(2)}) collective-permute-start(f32[4,64,256]{2,1,0:T(8,128)S(1)} %bitcast_add_fusion.2), channel_id=1, source_target_pairs={{128,160},{160,192},{192,224},{129,161},{161,193},{193,225},{130,1... | collective-permute-start | bytes 786440 | tf_op jit(solution)/shard_map/ppermute | solution.py:158
  218.0 8.3 %collective-permute-start.12 = (f32[4,64,256]{2,1,0:T(8,128)S(1)}, f32[4,64,256]{2,1,0:T(8,128)S(1)}, u32[]{:S(2)}, u32[]{:S(2)}) collective-permute-start(f32[4,64,256]{2,1,0:T(8,128)S(1)} %bitcast_add_fusion.1), channel_id=1, source_target_pairs={{160,192},{192,224},{161,193},{193,225},{162,194},{194,226},{163,1... | collective-permute-start | bytes 786440 | tf_op jit(solution)/shard_map/ppermute | solution.py:158
  226.4 8.3 %collective-permute-start.13 = (f32[4,64,256]{2,1,0:T(8,128)S(1)}, f32[4,64,256]{2,1,0:T(8,128)S(1)}, u32[]{:S(2)}, u32[]{:S(2)}) collective-permute-start(f32[4,64,256]{2,1,0:T(8,128)S(1)} %bitcast_add_fusion), channel_id=1, source_target_pairs={{192,224},{193,225},{194,226},{195,227},{196,228},{197,229},{198,2... | collective-permute-start | bytes 786440 | tf_op jit(solution)/shard_map/ppermute | solution.py:158
  (75 other events, 482.2 us)
Sparse Core Ops, SparseCore 0:
  48.3 78.8 all-reduce.1
where the time goes:
time: 253 us; the launch traced here: 252 us
  waiting for transfers between devices  113 us (45%)
  other arithmetic  49.7 us (20%)
  local copies, waits for them, and re-layouts  37.9 us (15%)
  matrix products  19.6 us (8%)
  between operations  18.3 us (7%)
  starting transfers between devices  13.8 us (5%)
    ppermute x10, waiting for transfers between devices, on_device(): got = lax.ppermute(sent, 'ctx', pairs)  62.1 us
    psum x1, waiting for transfers between devices, on_device(): picked = lax.psum(picked, 'ctx')  50.6 us
    unnamed x189, local copies, waits for them, and re-layouts  15.6 us
    convert_element_type x3, other arithmetic, causal_conv(): return jax.nn.silu(total).astype(jnp.bfloat16)  13.1 us
    ppermute x10, starting transfers between devices, on_device(): got = lax.ppermute(sent, 'ctx', pairs)  10.4 us
    dot_general x4, matrix products, block_output(): jnp.einsum('hqs,shp->qhp', weights, x_blk, preferred_element_type=jnp.flo...  7.94 us
    another operation x5, other arithmetic  6.93 us
  transfers between devices with their start and end apart: 15, of which 5 were waited for; matrix products, arithmetic and copies ran while one was open for 25% of the time, Pallas kernels for 0%

commit v1 on v0

--- a/solution.py
+++ b/solution.py
@@ -12,6 +12,18 @@
 STRETCH = 256
 CHUNKS = 4
 HIGHEST = lax.Precision.HIGHEST
+
+
+def _number_lots_all(device_axis, panel):
+    axis_len = lax.axis_size(device_axis)
+    f_next = panel
+    for to_i in [
+        [(tick, tick ^ dev) for tick in range(axis_len)]
+        for dev in (1, 2, 4, 8, 16)
+        if dev < axis_len
+    ]:
+        f_next = f_next + lax.ppermute(f_next, device_axis, perm=to_i)
+    return f_next
 
 
 def passed_along(value, axis, steps):
@@ -98,7 +110,7 @@
     conv_pick = jnp.where(on_chip, jnp.where(mine, conv_pool[0], other_conv), 0.0)
     picked = jnp.concatenate([state_pick.reshape(-1), conv_pick.reshape(-1)])
     picked, x_in, bc_in, dt_raw = lax.optimization_barrier((picked, x_in, bc_in, dt_raw))
-    picked = lax.psum(picked, "ctx")
+    picked = _number_lots_all("ctx", picked)
     first_state = picked[: state_pick.size].reshape(state_pick.shape)
     first_conv = picked[state_pick.size :].reshape(conv_pick.shape)
     tail_x = x_in[0, tokens - (K - 1) :, :]

time: 253 us -> 279 us (1.10)
  waiting for transfers between devices: 113 us -> 139 us
  between operations: 18.3 us -> 4.82 us
  starting transfers between devices: 13.8 us -> 23.4 us
  other arithmetic: 49.7 us -> 53 us
    ppermute x0 -> x3, waiting for transfers between devices: none -> 85.1 us  [_number_lots_all(): f_next = f_next + lax.ppermute(f_next, device_axis, perm=to_i)]
    psum x1 -> x0, waiting for transfers between devices: 50.6 us -> none  [on_device(): picked = lax.psum(picked, 'ctx')]
    ppermute x0 -> x3, starting transfers between devices: none -> 9.71 us  [_number_lots_all(): f_next = f_next + lax.ppermute(f_next, device_axis, perm=to_i)]
    ppermute x10, waiting for transfers between devices: 62.1 us -> 53.4 us  [on_device(): got = lax.ppermute(sent, 'ctx', pairs)]
    add x0 -> x3, other arithmetic: none -> 2.81 us  [_number_lots_all(): f_next = f_next + lax.ppermute(f_next, device_axis, perm=to_i)]
    unnamed x189 -> x185, local copies, waits for them, and re-layouts: 15.6 us -> 15.1 us
  transfers between devices with their start and end apart: 15 -> 17, of which waited for: 5 -> 6; matrix products, arithmetic and copies ran while one was open for 25% -> 27% of each run, Pallas kernels for 0% -> 0%
where the time goes in v1:
time: 279 us; the launch traced here: 278 us
  waiting for transfers between devices  139 us (50%)
  other arithmetic  53 us (19%)
  local copies, waits for them, and re-layouts  38.9 us (14%)
  starting transfers between devices  23.4 us (8%)
  matrix products  19.5 us (7%)
  between operations  4.82 us (2%)
    ppermute x3, waiting for transfers between devices, _number_lots_all(): f_next = f_next + lax.ppermute(f_next, device_axis, perm=to_i)  85.1 us
    ppermute x10, waiting for transfers between devices, on_device(): got = lax.ppermute(sent, 'ctx', pairs)  53.4 us
    unnamed x185, local copies, waits for them, and re-layouts  15.1 us
    convert_element_type x3, other arithmetic, causal_conv(): return jax.nn.silu(total).astype(jnp.bfloat16)  14.3 us
    ppermute x10, starting transfers between devices, on_device(): got = lax.ppermute(sent, 'ctx', pairs)  10.4 us
    ppermute x3, starting transfers between devices, _number_lots_all(): f_next = f_next + lax.ppermute(f_next, device_axis, perm=to_i)  9.71 us
    dot_general x4, matrix products, block_output(): jnp.einsum('hqs,shp->qhp', weights, x_blk, preferred_element_type=jnp.flo...  7.9 us
    another operation x5, other arithmetic  6.93 us
  transfers between devices with their start and end apart: 17, of which 6 were waited for; matrix products, arithmetic and copies ran while one was open for 27% of the time, Pallas kernels for 0%

profile of v1, /device:TPU:232, one launch (start us, length us, event | category | flops | bytes accessed | tf_op | source)
XLA Modules:
  0.0 278.1 jit_solution(10979423517994858920)
XLA Ops:
  12.4 3.9 %copy.78 = bf16[1,1024,1024]{1,2,0:T(8,128)(2,1)} copy(bf16[1,1024,1024]{2,1,0:T(8,128)(2,1)} %param.16) | data formatting | bytes 4194304 | tf_op args[2]
  22.5 2.9 %copy.66 = bf16[1,1024,1024]{1,2,0:T(8,128)(2,1)S(1)} copy(bf16[1,1024,1024]{2,1,0:T(8,128)(2,1)} %param.14) | data formatting | bytes 4194304 | tf_op jit(solution)/shard_map/optimization_barrier | solution.py:112
  27.0 2.3 reduce-window.14
  35.6 2.6 collective-permute-start.2
  39.6 3.0 %fusion.21 = f32[1021,1024]{0,1:T(8,128)} fusion(bf16[1,1024,1024]{1,2,0:T(8,128)(2,1)S(1)} %copy.66), kind=kLoop, calls=%fused_computation.38 | loop fusion | flops 1045504 | bytes 6273024 | tf_op jit(solution)/shard_map/convert_element_type | solution.py:36
  44.7 4.5 %reduce-window.16 = f32[16,8,128]{2,1,0:T(8,128)S(1)} reduce-window(f32[16,8,128]{2,1,0:T(8,128)S(1)} %fusion.116, f32[]{:T(128)} %constant.162.clone.1), window={size=1x1x128 pad=0_0x0_0x127_0}, to_apply=%region_3.4 | reduce-window | flops 2080768 | bytes 131076 | tf_op jit(solution)/shard_map/reduce-window.2
  51.3 11.2 %multiply_convert_fusion.4 = bf16[1021,1024]{0,1:T(8,128)(2,1)S(1)} fusion(f32[1021,1024]{0,1:T(8,128)} %fusion.21, f32[3,1024]{0,1:T(8,128)} %copy.67, f32[1024]{0:T(1024)S(1)} %bitcast.440, f32[1024]{0:T(1024)S(1)} %bitcast.442, f32[1024]{0:T(1024)S(1)} %bitcast.438, f32[1024]{0:T(1024)S(1)} %bitcast.436), kind=kLoop, calls=%fused_computation.24 | loop fusion | flops 15682560 | bytes 6301696 | tf_op jit(solution)/shard_map/convert_element_type | solution.py:41
  62.5 1.9 fusion.148
  65.8 2.2 collective-permute-start.3
  72.2 42.2 %collective-permute-done.3 = f32[265216]{0:T(1024)} collective-permute-done((f32[265216]{0:T(1024)S(1)}, f32[265216]{0:T(1024)}, u32[]{:S(2)}, u32[]{:S(2)}) %collective-permute-start.3) | collective-permute-done | bytes 1060896 | tf_op jit(solution)/shard_map/ppermute | solution.py:25
  115.8 4.9 %collective-permute-start.4 = (f32[265216]{0:T(1024)S(1)}, f32[265216]{0:T(1024)S(1)}, u32[]{:S(2)}, u32[]{:S(2)}) collective-permute-start(f32[265216]{0:T(1024)S(1)} %add.291), channel_id=1, source_target_pairs={{0,128},{32,160},{64,192},{96,224},{128,0},{160,32},{192,64},{224,... | collective-permute-start | bytes 3182600 | tf_op jit(solution)/shard_map/ppermute | solution.py:25
  121.0 2.4 multiply_convert_fusion.9
  124.5 42.9 %collective-permute-done.4 = f32[265216]{0:T(1024)S(1)} collective-permute-done((f32[265216]{0:T(1024)S(1)}, f32[265216]{0:T(1024)S(1)}, u32[]{:S(2)}, u32[]{:S(2)}) %collective-permute-start.4) | collective-permute-done | bytes 1060896 | tf_op jit(solution)/shard_map/ppermute | solution.py:25
  170.1 2.9 %fusion.65 = (bf16[256,1024]{0,1:T(8,128)(2,1)S(1)}, bf16[256,1024]{0,1:T(8,128)(2,1)}, bf16[256,1024]{0,1:T(8,128)(2,1)S(1)}, bf16[256,1024]{0,1:T(8,128)(2,1)S(1)}, bf16[256,1024]{0,1:T(8,128)(2,1)S(1)}) fusion(f32[256,16]{0,1:T(8,128)S(1)} %get-tuple-element.52, bf16[1021,1024]{0,1:T(8,128)(2,1)S(1)} %multiply_convert_fusion.4, ...), kind=kLoop, calls=%fused_computation.94 | loop fusion | flops 4194304 | bytes 6619136 | tf_op jit(solution)/shard_map/convert_element_type | solution.py:50
  176.2 2.5 reshape_reshape.3
  178.8 2.1 multiply_add_fusion
  184.2 2.6 fusion.47
  187.9 2.6 fusion.46
  199.6 2.5 slice.267
  206.6 28.6 %collective-permute-done.13 = f32[4,64,256]{2,1,0:T(8,128)S(1)} collective-permute-done((f32[4,64,256]{2,1,0:T(8,128)S(1)}, f32[4,64,256]{2,1,0:T(8,128)S(1)}, u32[]{:S(2)}, u32[]{:S(2)}) %collective-permute-start.13) | collective-permute-done | bytes 262176 | tf_op jit(solution)/shard_map/ppermute | solution.py:170
  239.1 10.0 %collective-permute-done.14 = f32[4,64,256]{2,1,0:T(8,128)S(1)} collective-permute-done((f32[4,64,256]{2,1,0:T(8,128)S(1)}, f32[4,64,256]{2,1,0:T(8,128)S(1)}, u32[]{:S(2)}, u32[]{:S(2)}) %collective-permute-start.14) | collective-permute-done | bytes 262176 | tf_op jit(solution)/shard_map/ppermute | solution.py:170
  251.5 7.9 %collective-permute-done.15 = f32[4,64,256]{2,1,0:T(8,128)S(1)} collective-permute-done((f32[4,64,256]{2,1,0:T(8,128)S(1)}, f32[4,64,256]{2,1,0:T(8,128)S(1)}, u32[]{:S(2)}, u32[]{:S(2)}) %collective-permute-start.15) | collective-permute-done | bytes 262176 | tf_op jit(solution)/shard_map/ppermute | solution.py:170
  260.9 6.9 %collective-permute-done.16 = f32[4,64,256]{2,1,0:T(8,128)S(1)} collective-permute-done((f32[4,64,256]{2,1,0:T(8,128)S(1)}, f32[4,64,256]{2,1,0:T(8,128)S(1)}, u32[]{:S(2)}, u32[]{:S(2)}) %collective-permute-start.16) | collective-permute-done | bytes 262176 | tf_op jit(solution)/shard_map/ppermute | solution.py:170
  275.6 2.6 copy.79
  (307 shorter events, 75.3 us)
Async XLA Ops:
  0.7 15.8 %collective-permute-start = (f32[16,64,256]{2,1,0:T(8,128)}, f32[16,64,256]{2,1,0:T(8,128)S(1)}, u32[]{:S(2)}, u32[]{:S(2)}) collective-permute-start(f32[16,64,256]{2,1,0:T(8,128)} %bitcast.416), channel_id=1, source_target_pairs={{0,1},{1,0},{2,3},{3,2},{4,5},{5,4},{6,7},{7,6},{8,9},{9,8},{10,11... | collective-permute-start | bytes 3145736 | tf_op jit(solution)/shard_map/ppermute | solution.py:108
  1.5 14.9 %collective-permute-start.1 = (f32[3,1024]{1,0:T(4,128)S(1)}, f32[3,1024]{1,0:T(4,128)S(1)}, u32[]{:S(2)}, u32[]{:S(2)}) collective-permute-start(f32[3,1024]{1,0:T(4,128)S(1)} %bitcast.445), channel_id=1, source_target_pairs={{0,1},{1,0},{2,3},{3,2},{4,5},{5,4},{6,7},{7,6},{8,9},{9,8},{10,11... | collective-permute-start | bytes 36872 | tf_op jit(solution)/shard_map/ppermute | solution.py:108
  25.4 45.9 %collective-permute-start.6 = (bf16[3,4096]{1,0:T(4,128)(2,1)}, bf16[3,4096]{1,0:T(4,128)(2,1)}, u32[]{:S(2)}, u32[]{:S(2)}) collective-permute-start(bf16[3,4096]{1,0:T(4,128)(2,1)} %slice_bitcast_fusion.3), channel_id=1, source_target_pairs={{0,32},{32,64},{64,96},{96,128},{128,160},{160,192},{192,224},{1,3... | collective-permute-start | bytes 73736 | tf_op jit(solution)/shard_map/ppermute | solution.py:32
  35.6 28.9 %collective-permute-start.2 = (f32[265216]{0:T(1024)}, f32[265216]{0:T(1024)}, u32[]{:S(2)}, u32[]{:S(2)}) collective-permute-start(f32[265216]{0:T(1024)} %pad_maximum_fusion.2), channel_id=1, source_target_pairs={{0,32},{32,0},{64,96},{96,64},{128,160},{160,128},{192,224},{224,1... | collective-permute-start | bytes 3182600 | tf_op jit(solution)/shard_map/ppermute | solution.py:25
  38.2 130.3 %collective-permute-start.5 = (bf16[3,1024]{1,0:T(4,128)(2,1)}, bf16[3,1024]{1,0:T(4,128)(2,1)S(1)}, u32[]{:S(2)}, u32[]{:S(2)}) collective-permute-start(bf16[3,1024]{1,0:T(4,128)(2,1)} %get-tuple-element.35), channel_id=1, source_target_pairs={{0,32},{32,64},{64,96},{96,128},{128,160},{160,192},{192,224},{1,3... | collective-permute-start | bytes 18440 | tf_op jit(solution)/shard_map/ppermute | solution.py:32
  65.8 55.2 %copy-start.57 = (f32[1,512]{1,0:T(1,128)S(1)}, f32[1,512]{1,0:T(1,128)}, u32[]{:S(2)}) copy-start(f32[1,512]{1,0:T(1,128)} %get-tuple-element.63) | copy-start | bytes 6148
  65.8 55.2 %copy-start.58 = (f32[1,512]{1,0:T(1,128)S(1)}, f32[1,512]{1,0:T(1,128)}, u32[]{:S(2)}) copy-start(f32[1,512]{1,0:T(1,128)} %get-tuple-element.64) | copy-start | bytes 6148
  65.8 55.2 %copy-start.59 = (f32[1,512]{1,0:T(1,128)S(1)}, f32[1,512]{1,0:T(1,128)}, u32[]{:S(2)}) copy-start(f32[1,512]{1,0:T(1,128)} %get-tuple-element.65) | copy-start | bytes 6148
  65.8 55.2 %copy-start.60 = (f32[1,512]{1,0:T(1,128)S(1)}, f32[1,512]{1,0:T(1,128)}, u32[]{:S(2)}) copy-start(f32[1,512]{1,0:T(1,128)} %get-tuple-element.66) | copy-start | bytes 6148
  65.8 48.6 %collective-permute-start.3 = (f32[265216]{0:T(1024)S(1)}, f32[265216]{0:T(1024)}, u32[]{:S(2)}, u32[]{:S(2)}) collective-permute-start(f32[265216]{0:T(1024)S(1)} %add.290), channel_id=1, source_target_pairs={{0,64},{32,96},{64,0},{96,32},{128,192},{160,224},{192,128},{224,1... | collective-permute-start | bytes 3182600 | tf_op jit(solution)/shard_map/ppermute | solution.py:25
  115.8 51.5 %collective-permute-start.4 = (f32[265216]{0:T(1024)S(1)}, f32[265216]{0:T(1024)S(1)}, u32[]{:S(2)}, u32[]{:S(2)}) collective-permute-start(f32[265216]{0:T(1024)S(1)} %add.291), channel_id=1, source_target_pairs={{0,128},{32,160},{64,192},{96,224},{128,0},{160,32},{192,64},{224,... | collective-permute-start | bytes 3182600 | tf_op jit(solution)/shard_map/ppermute | solution.py:25
  123.4 51.5 %copy-start.4 = (bf16[1024,512]{1,0:T(8,128)(2,1)}, bf16[1024,512]{1,0:T(8,128)(2,1)S(1)}, u32[]{:S(2)}) copy-start(bf16[1024,512]{1,0:T(8,128)(2,1)S(1)} %multiply_convert_fusion.9) | copy-start | bytes 3145732
  181.0 2.4 collective-permute-start.7
  183.5 3.5 %collective-permute-start.8 = (f32[4,64,256]{2,1,0:T(8,128)S(1)}, f32[4,64,256]{2,1,0:T(8,128)S(1)}, u32[]{:S(2)}, u32[]{:S(2)}) collective-permute-start(f32[4,64,256]{2,1,0:T(8,128)S(1)} %bitcast_add_fusion.8), channel_id=1, source_target_pairs={{0,32},{32,64},{1,33},{33,65},{2,34},{34,66},{3,35},{35,67},{4,36}... | collective-permute-start | bytes 786440 | tf_op jit(solution)/shard_map/ppermute | solution.py:170
  187.1 3.5 %collective-permute-start.9 = (f32[4,64,256]{2,1,0:T(8,128)S(1)}, f32[4,64,256]{2,1,0:T(8,128)S(1)}, u32[]{:S(2)}, u32[]{:S(2)}) collective-permute-start(f32[4,64,256]{2,1,0:T(8,128)S(1)} %bitcast_add_fusion.7), channel_id=1, source_target_pairs={{0,32},{32,64},{64,96},{1,33},{33,65},{65,97},{2,34},{34,66},{66,9... | collective-permute-start | bytes 786440 | tf_op jit(solution)/shard_map/ppermute | solution.py:170
  190.8 2.2 collective-permute-start.10
  193.1 2.5 collective-permute-start.11
  196.5 5.7 %collective-permute-start.12 = (f32[4,64,256]{2,1,0:T(8,128)}, f32[4,64,256]{2,1,0:T(8,128)}, u32[]{:S(2)}, u32[]{:S(2)}) collective-permute-start(f32[4,64,256]{2,1,0:T(8,128)} %bitcast_add_fusion.4), channel_id=1, source_target_pairs={{64,96},{96,128},{128,160},{160,192},{65,97},{97,129},{129,161},{1... | collective-permute-start | bytes 786440 | tf_op jit(solution)/shard_map/ppermute | solution.py:170
  197.9 51.3 %copy-start.71 = (f32[4]{0:T(128)S(1)}, f32[4]{0:T(128)}, u32[]{:S(2)}) copy-start(f32[4]{0:T(128)} %get-tuple-element.68) | copy-start | bytes 52
  199.6 59.9 %copy-start.70 = (f32[4]{0:T(128)S(1)}, f32[4]{0:T(128)}, u32[]{:S(2)}) copy-start(f32[4]{0:T(128)} %get-tuple-element.67) | copy-start | bytes 52
  203.4 31.8 %collective-permute-start.13 = (f32[4,64,256]{2,1,0:T(8,128)S(1)}, f32[4,64,256]{2,1,0:T(8,128)S(1)}, u32[]{:S(2)}, u32[]{:S(2)}) collective-permute-start(f32[4,64,256]{2,1,0:T(8,128)S(1)} %bitcast_add_fusion.3), channel_id=1, source_target_pairs={{96,128},{128,160},{160,192},{192,224},{97,129},{129,161},{161,193... | collective-permute-start | bytes 786440 | tf_op jit(solution)/shard_map/ppermute | solution.py:170
  236.3 12.8 %collective-permute-start.14 = (f32[4,64,256]{2,1,0:T(8,128)S(1)}, f32[4,64,256]{2,1,0:T(8,128)S(1)}, u32[]{:S(2)}, u32[]{:S(2)}) collective-permute-start(f32[4,64,256]{2,1,0:T(8,128)S(1)} %bitcast_add_fusion.2), channel_id=1, source_target_pairs={{128,160},{160,192},{192,224},{129,161},{161,193},{193,225},{130,1... | collective-permute-start | bytes 786440 | tf_op jit(solution)/shard_map/ppermute | solution.py:170
  249.2 10.2 %collective-permute-start.15 = (f32[4,64,256]{2,1,0:T(8,128)S(1)}, f32[4,64,256]{2,1,0:T(8,128)S(1)}, u32[]{:S(2)}, u32[]{:S(2)}) collective-permute-start(f32[4,64,256]{2,1,0:T(8,128)S(1)} %bitcast_add_fusion.1), channel_id=1, source_target_pairs={{160,192},{192,224},{161,193},{193,225},{162,194},{194,226},{163,1... | collective-permute-start | bytes 786440 | tf_op jit(solution)/shard_map/ppermute | solution.py:170
  259.5 8.3 %collective-permute-start.16 = (f32[4,64,256]{2,1,0:T(8,128)S(1)}, f32[4,64,256]{2,1,0:T(8,128)S(1)}, u32[]{:S(2)}, u32[]{:S(2)}) collective-permute-start(f32[4,64,256]{2,1,0:T(8,128)S(1)} %bitcast_add_fusion), channel_id=1, source_target_pairs={{192,224},{193,225},{194,226},{195,227},{196,228},{197,229},{198,2... | collective-permute-start | bytes 786440 | tf_op jit(solution)/shard_map/ppermute | solution.py:170
  (75 other events, 776.2 us)
